TPU v7x, 256 devices: a whole 4x4x8 slice. The times are simulated.
256 devices in a mesh: sub: 64 (over z, x, core), row: 4 (over y).
Axes of the slice: x: 4, y: 4, z: 8, core: 2. Of those that a mesh axis runs over, the one named last changes fastest.
Arguments:
- residual: float32 [32, 64, 2048], P(None, 'sub', 'row')
- factor: float32 [64, 3072, 3072], P('sub', 'row'), may hold values from -0.0390625 to 0.0390625
- basis: float32 [96, 64, 2048], P(None, 'sub', 'row'), may hold values from -0.015625 to 0.015625
- send_rows: int32 [64, 2, 512], P('sub'), may hold values from 0 to 2047, as said below
Outputs:
- coeffs: float32 [96, 32], replicated
- rfactor: float32 [32, 32], replicated
- block_q: float32 [32, 64, 2048], P(None, 'sub', 'row')
Inputs may be any that keep to these rules, and one draw needn't show every extreme that they name: Within each send_rows[s, side, :] the rows are distinct.
All inputs are finite; a program needn't handle non-finite values.
Results may differ from a plain program's by a relative error of at most 0.000073.
Values sent between devices are 32-bit elements; how exact they have to be, the bound alone decides.
No kernel may reach another device: no remote copies, remote signals or barrier semaphores. Data moves between devices by JAX's collectives and lax.ppermute only.
A program may use at most 64 MiB of HBM per device.

v0:
```python
import jax
import jax.numpy as jnp
from jax import lax
from jax.sharding import PartitionSpec as P

HIGH = lax.Precision.HIGHEST


def from_behind(value, axis, steps):
    count = lax.axis_size(axis)
    leading, last = (max(0, -steps), min(count, count - steps))
    return lax.ppermute(value, axis, [(source, source + steps) for source in range(leading, last)])


def contract_rows(left_mat, right_mat):
    return lax.dot_general(left_mat, right_mat, (((1,), (1,)), ((), ())), precision=HIGH)


def contract_first(left_mat, right_mat):
    return lax.dot_general(left_mat, right_mat, (((0,), (0,)), ((), ())), precision=HIGH)


def second_sum(inner):
    return lax.psum(inner, ("sub", "row"))


def per_device(residual, factor, basis, send_rows):
    slab = residual.shape[2]
    row_count = lax.axis_size("row")
    sub_rows = slab * row_count
    total_rows = sub_rows * lax.axis_size("sub")
    own_rows = residual[:, 0, :]
    whole = lax.all_gather(own_rows, "row", axis=1, tiled=True)
    index_rows = send_rows[0]
    to_lower = jnp.take(whole, index_rows[0], axis=1)
    to_upper = jnp.take(whole, index_rows[1], axis=1)
    from_lower = from_behind(to_upper, "sub", 1)
    from_upper = from_behind(to_lower, "sub", -1)
    extended = jnp.concatenate([whole, from_lower, from_upper], axis=1)
    factor_rows = factor[0]
    share = factor_rows.shape[0]
    margin = from_lower.shape[1]
    row_pos = lax.axis_index("row")
    global_rows = row_pos * share + lax.iota(jnp.int32, share)
    columns = lax.iota(jnp.int32, factor_rows.shape[1])
    full = factor_rows + (global_rows[:, None] == columns[None, :]).astype(jnp.float32)
    inner = contract_rows(extended, full)
    partial_value = jnp.dot(inner, full, precision=HIGH)
    summed = lax.psum(partial_value, "row")
    mine = lax.dynamic_slice_in_dim(summed, row_pos * slab, slab, 1)
    margins = summed[:, sub_rows:]
    back_upper = from_behind(margins[:, :margin], "sub", -1)
    back_lower = from_behind(margins[:, margin:], "sub", 1)
    my_rows = row_pos * slab + lax.iota(jnp.int32, slab)
    select_upper = (index_rows[1][:, None] == my_rows[None, :]).astype(jnp.float32)
    select_lower = (index_rows[0][:, None] == my_rows[None, :]).astype(jnp.float32)
    block_t = (
        mine
        + jnp.dot(back_upper, select_upper, precision=HIGH)
        + jnp.dot(back_lower, select_lower, precision=HIGH)
    )
    vectors = basis[:, 0, :]
    first = lax.psum(contract_rows(vectors, block_t), ("sub", "row"))
    once = block_t - contract_first(first, vectors)
    inner_two = contract_rows(vectors, once)
    second = second_sum(inner_two)
    twice = once - contract_first(second, vectors)
    gram = lax.psum(contract_rows(twice, twice), ("sub", "row")) / total_rows
    lower_tri = jnp.linalg.cholesky(gram)
    solved = jax.scipy.linalg.solve_triangular(lower_tri, twice, lower=True)
    return (first + second, lower_tri.T, solved[:, None, :])


def solution(mesh):
    placed = (
        P(None, "sub", "row"),
        P("sub", "row", None),
        P(None, "sub", "row"),
        P("sub", None, None),
    )
    return jax.shard_map(
        per_device,
        mesh=mesh,
        in_specs=placed,
        out_specs=(P(), P(), P(None, "sub", "row")),
        check_vma=False,
    )
```

profile of v0, /device:TPU:1, one launch (start us, length us, event | category | flops | bytes accessed | tf_op | source)
XLA Modules:
  0.0 366.8 jit_solution(2224883184185922251)
XLA Ops:
  7.2 0.8 fusion.30
  8.0 1.0 copy.12
  9.0 14.5 %all-gather = f32[32,1,2048]{0,2,1:T(8,128)S(1)} all-gather(f32[32,1,512]{0,2,1:T(8,128)S(1)} %copy.12), channel_id=2, replica_groups=mesh['sub'=64,'row'=4] {'row'}, dimensions={2}, use_global_device_ids=true | all-gather | bytes 327680 | tf_op jit(solution)/shard_map/all_gather | solution.py:33
  23.5 1.0 gather_fusion
  24.6 5.2 %collective-permute-start = (f32[32,512]{0,1:T(8,128)S(1)}, f32[32,512]{0,1:T(8,128)S(1)}, u32[]{:S(2)}, u32[]{:S(2)}) collective-permute-start(f32[32,512]{0,1:T(8,128)S(1)} %select_bitcast_fusion.1), channel_id=1, source_target_pairs={{0,4},{4,8},{8,12},{12,16},{16,20},{20,24},{24,28},{28,32},{32,36}... | collective-permute-start | bytes 196616 | tf_op jit(solution)/shard_map/ppermute | solution.py:12
  29.8 1.0 gather_fusion.1
  31.0 1.9 collective-permute-start.1
  33.4 5.3 %collective-permute-done.1 = f32[32,512]{0,1:T(8,128)S(1)} collective-permute-done((f32[32,512]{0,1:T(8,128)S(1)}, f32[32,512]{0,1:T(8,128)S(1)}, u32[]{:S(2)}, u32[]{:S(2)}) %collective-permute-start.1) | collective-permute-done | bytes 65568 | tf_op jit(solution)/shard_map/ppermute | solution.py:12
  38.8 11.7 %fusion.1 = f32[32,768]{1,0:T(8,128)S(1)} fusion(f32[1,768,3072]{2,1,0:T(8,128)} %param.7, s32[768]{0:T(1024)S(1)} %iota_add_fusion, f32[32,512]{1,0:T(8,128)S(1)} %copy.15, f32[32,512]{1,0:T(8,128)S(1)} %copy.14, f32[32,2048]{1,0:T(8,128)S(1)} %copy.13), kind=kOutput, calls=%fused_computation.5 | convolution fusion | flops 913244160 | bytes 9931776 | tf_op jit(solution)/shard_map/dot_general | solution.py:16
  50.6 7.4 %fusion = f32[32,3072]{1,0:T(8,128)} fusion(f32[32,768]{1,0:T(8,128)S(1)} %fusion.1, f32[1,768,3072]{2,1,0:T(8,128)S(1)} %copy-done, s32[768]{0:T(1024)S(1)} %iota_add_fusion), kind=kOutput, calls=%fused_computation.4 | convolution fusion | flops 913047552 | bytes 9931776 | tf_op jit(solution)/shard_map/dot_general | solution.py:48
  58.0 50.1 %all-reduce.2.cloned.1.call-done = f32[32,3072]{1,0:T(8,128)} async-done(((f32[32,3072]{1,0:T(8,128)}), f32[32,3072]{1,0:T(8,128)}) %all-reduce.2.cloned.1.call-update) | async-done | bytes 393232 | tf_op jit(solution)/shard_map/psum | solution.py:49
  108.2 0.9 fusion.29
  109.1 5.8 %collective-permute-start.3 = (f32[32,512]{1,0:T(8,128)S(1)}, f32[32,512]{1,0:T(8,128)S(1)}, u32[]{:S(2)}, u32[]{:S(2)}) collective-permute-start(f32[32,512]{1,0:T(8,128)S(1)} %get-tuple-element.11), channel_id=1, source_target_pairs={{0,4},{4,8},{8,12},{12,16},{16,20},{20,24},{24,28},{28,32},{32,36}... | collective-permute-start | bytes 196616 | tf_op jit(solution)/shard_map/ppermute | solution.py:12
  114.9 2.1 collective-permute-start.2
  117.5 3.0 collective-permute-done.2
  120.5 1.4 fusion.4
  122.2 80.5 %psum.29 = f32[96,32]{0,1:T(8,128)S(1)} all-reduce(f32[96,32]{0,1:T(8,128)S(1)} %convolution_bitcast_fusion.2), channel_id=1, replica_groups=mesh['sub'=64,'row'=4] {'sub','row'}, use_global_device_ids=true, to_apply=%region_1.3 | all-reduce | flops 3072 | bytes 24576 | tf_op jit(solution)/shard_map/psum | solution.py:63
  203.3 72.9 %psum.30 = f32[96,32]{0,1:T(8,128)S(1)} all-reduce(f32[96,32]{0,1:T(8,128)S(1)} %convolution_bitcast_fusion.1), channel_id=1, replica_groups=mesh['sub'=64,'row'=4] {'sub','row'}, use_global_device_ids=true, to_apply=%region_2.4 | all-reduce | flops 3072 | bytes 24576 | tf_op jit(solution)/shard_map/psum | solution.py:24
  277.2 74.4 %psum.31 = f32[32,32]{0,1:T(8,128)S(1)} all-reduce(f32[32,32]{0,1:T(8,128)S(1)} %fusion.31), channel_id=1, replica_groups=mesh['sub'=64,'row'=4] {'sub','row'}, use_global_device_ids=true, to_apply=%region_3.5 | all-reduce | flops 1024 | bytes 8192 | tf_op jit(solution)/shard_map/psum | solution.py:68
  351.6 2.9 cholesky.18
  355.2 0.7 select_bitcast_fusion.2
  355.9 2.4 custom-call.7
  358.6 0.7 copy.19
  359.3 0.7 copy.18
  (34 shorter events, 4.3 us)
Async XLA Ops:
  7.2 101.0 %all-reduce.2.cloned.1.call-start = ((), (), s32[]{:S(2)}) async-start(), calls=%async_computation | async-start | bytes 786432 | tf_op jit(solution)/shard_map/psum | solution.py:49
  24.6 8.6 %collective-permute-start = (f32[32,512]{0,1:T(8,128)S(1)}, f32[32,512]{0,1:T(8,128)S(1)}, u32[]{:S(2)}, u32[]{:S(2)}) collective-permute-start(f32[32,512]{0,1:T(8,128)S(1)} %select_bitcast_fusion.1), channel_id=1, source_target_pairs={{0,4},{4,8},{8,12},{12,16},{16,20},{20,24},{24,28},{28,32},{32,36}... | collective-permute-start | bytes 196616 | tf_op jit(solution)/shard_map/ppermute | solution.py:12
  31.0 7.7 %collective-permute-start.1 = (f32[32,512]{0,1:T(8,128)S(1)}, f32[32,512]{0,1:T(8,128)S(1)}, u32[]{:S(2)}, u32[]{:S(2)}) collective-permute-start(f32[32,512]{0,1:T(8,128)S(1)} %select_bitcast_fusion), channel_id=1, source_target_pairs={{4,0},{8,4},{12,8},{16,12},{20,16},{24,20},{28,24},{32,28},{36,32}... | collective-permute-start | bytes 196616 | tf_op jit(solution)/shard_map/ppermute | solution.py:12
  38.8 11.8 %copy-start = (f32[1,768,3072]{2,1,0:T(8,128)S(1)}, f32[1,768,3072]{2,1,0:T(8,128)}, u32[]{:S(2)}) copy-start(f32[1,768,3072]{2,1,0:T(8,128)} %param.7) | copy-start | bytes 28311556
  38.8 83.0 %copy-start.1 = (f32[96,1,512]{2,1,0:T(1,128)S(1)}, f32[96,1,512]{2,1,0:T(1,128)}, u32[]{:S(2)}) copy-start(f32[96,1,512]{2,1,0:T(1,128)} %param.8) | copy-start | bytes 589828
  109.1 8.0 %collective-permute-start.3 = (f32[32,512]{1,0:T(8,128)S(1)}, f32[32,512]{1,0:T(8,128)S(1)}, u32[]{:S(2)}, u32[]{:S(2)}) collective-permute-start(f32[32,512]{1,0:T(8,128)S(1)} %get-tuple-element.11), channel_id=1, source_target_pairs={{0,4},{4,8},{8,12},{12,16},{16,20},{20,24},{24,28},{28,32},{32,36}... | collective-permute-start | bytes 196616 | tf_op jit(solution)/shard_map/ppermute | solution.py:12
  114.9 5.6 %collective-permute-start.2 = (f32[32,512]{1,0:T(8,128)S(1)}, f32[32,512]{1,0:T(8,128)S(1)}, u32[]{:S(2)}, u32[]{:S(2)}) collective-permute-start(f32[32,512]{1,0:T(8,128)S(1)} %get-tuple-element.10), channel_id=1, source_target_pairs={{4,0},{8,4},{12,8},{16,12},{20,16},{24,20},{28,24},{32,28},{36,32}... | collective-permute-start | bytes 196616 | tf_op jit(solution)/shard_map/ppermute | solution.py:12
Sparse Core Ops, SparseCore 0:
  58.2 49.9 all-reduce.1
where the time goes:
time: 368 us; the launch traced here: 367 us
  blocking collectives  242 us (66%)
  waiting for transfers between devices  58.4 us (16%)
  matrix products  22.6 us (6%)
  starting transfers between devices  15 us (4%)
  between operations  14.3 us (4%)
  other arithmetic  7.62 us (2%)
  local copies, waits for them, and re-layouts  6.65 us (2%)
    psum x1, blocking collectives, per_device(): first = lax.psum(contract_rows(vectors, block_t), ('sub', 'row'))  80.5 us
    psum x1, blocking collectives, per_device(): gram = lax.psum(contract_rows(twice, twice), ('sub', 'row')) / total_rows  74.4 us
    psum x1, blocking collectives, second_sum(): return lax.psum(inner, ('sub', 'row'))  72.9 us
    psum x1, waiting for transfers between devices, per_device(): summed = lax.psum(partial_value, 'row')  50.1 us
    ppermute x4, starting transfers between devices, from_behind(): lax.ppermute(value, axis, [(source, source + steps) for source in range(l...  15 us
    all_gather x1, blocking collectives, per_device(): whole = lax.all_gather(own_rows, 'row', axis=1, tiled=True)  14.5 us
    dot_general x4, matrix products, contract_rows(): lax.dot_general(left_mat, right_mat, (((1,), (1,)), ((), ())), precision=...  12.6 us
    ppermute x4, waiting for transfers between devices, from_behind(): lax.ppermute(value, axis, [(source, source + steps) for source in range(l...  8.3 us
  transfers between devices with their start and end apart: 5, of which 3 were waited for; matrix products, arithmetic and copies ran while one was open for 1% of the time, Pallas kernels for 0%

commit v1 on v0

--- a/solution.py
+++ b/solution.py
@@ -1,9 +1,18 @@
+import functools
 import jax
 import jax.numpy as jnp
 from jax import lax
 from jax.sharding import PartitionSpec as P
 
 HIGH = lax.Precision.HIGHEST
+
+
+def view_the_bars(xin, group_axis):
+    tall = jax.lax.all_gather(xin, group_axis)
+    return jnp.sum(tall, 0)
+
+
+wrap_the_field = functools.partial(view_the_bars, group_axis=("sub", "row"))
 
 
 def from_behind(value, axis, steps):
@@ -65,7 +74,7 @@
     inner_two = contract_rows(vectors, once)
     second = second_sum(inner_two)
     twice = once - contract_first(second, vectors)
-    gram = lax.psum(contract_rows(twice, twice), ("sub", "row")) / total_rows
+    gram = wrap_the_field(contract_rows(twice, twice)) / total_rows
     lower_tri = jnp.linalg.cholesky(gram)
     solved = jax.scipy.linalg.solve_triangular(lower_tri, twice, lower=True)
     return (first + second, lower_tri.T, solved[:, None, :])

time: 368 us -> 409 us (1.11)
  waiting for transfers between devices: 58.4 us -> 171 us
  blocking collectives: 242 us -> 168 us
    all_gather x0 -> x1, waiting for transfers between devices: none -> 113 us  [view_the_bars(): tall = jax.lax.all_gather(xin, group_axis)]
    psum x1 -> x0, blocking collectives: 74.4 us -> none  [per_device(): gram = lax.psum(contract_rows(twice, twice), ('sub', 'row')) / total_rows]
  transfers between devices with their start and end apart: 5 -> 6, of which waited for: 3 -> 4; matrix products, arithmetic and copies ran while one was open for 1% -> 1% of each run, Pallas kernels for 0% -> 0%
where the time goes in v1:
time: 409 us; the launch traced here: 408 us
  waiting for transfers between devices  171 us (42%)
  blocking collectives  168 us (41%)
  matrix products  23.2 us (6%)
  starting transfers between devices  15.1 us (4%)
  between operations  14.3 us (3%)
  other arithmetic  10.1 us (2%)
  local copies, waits for them, and re-layouts  6.64 us (2%)
    all_gather x1, waiting for transfers between devices, view_the_bars(): tall = jax.lax.all_gather(xin, group_axis)  113 us
    psum x1, blocking collectives, per_device(): first = lax.psum(contract_rows(vectors, block_t), ('sub', 'row'))  80.5 us
    psum x1, blocking collectives, second_sum(): return lax.psum(inner, ('sub', 'row'))  72.9 us
    psum x1, waiting for transfers between devices, per_device(): summed = lax.psum(partial_value, 'row')  50.1 us
    ppermute x4, starting transfers between devices, from_behind(): lax.ppermute(value, axis, [(source, source + steps) for source in range(l...  15 us
    all_gather x1, blocking collectives, per_device(): whole = lax.all_gather(own_rows, 'row', axis=1, tiled=True)  14.5 us
    dot_general x4, matrix products, contract_rows(): lax.dot_general(left_mat, right_mat, (((1,), (1,)), ((), ())), precision=...  13.2 us
    ppermute x4, waiting for transfers between devices, from_behind(): lax.ppermute(value, axis, [(source, source + steps) for source in range(l...  8.29 us
  transfers between devices with their start and end apart: 6, of which 4 were waited for; matrix products, arithmetic and copies ran while one was open for 1% of the time, Pallas kernels for 0%

profile of v1, /device:TPU:1, one launch (start us, length us, event | category | flops | bytes accessed | tf_op | source)
XLA Modules:
  0.0 408.1 jit_solution(868761952216870104)
XLA Ops:
  7.2 0.8 fusion.30
  8.0 1.0 copy.11
  9.0 14.5 %all-gather = f32[32,1,2048]{0,2,1:T(8,128)S(1)} all-gather(f32[32,1,512]{0,2,1:T(8,128)S(1)} %copy.11), channel_id=2, replica_groups=mesh['sub'=64,'row'=4] {'row'}, dimensions={2}, use_global_device_ids=true | all-gather | bytes 327680 | tf_op jit(solution)/shard_map/all_gather | solution.py:42
  23.5 1.0 gather_fusion
  24.6 5.2 %collective-permute-start = (f32[32,512]{0,1:T(8,128)S(1)}, f32[32,512]{0,1:T(8,128)S(1)}, u32[]{:S(2)}, u32[]{:S(2)}) collective-permute-start(f32[32,512]{0,1:T(8,128)S(1)} %select_bitcast_fusion.1), channel_id=1, source_target_pairs={{0,4},{4,8},{8,12},{12,16},{16,20},{20,24},{24,28},{28,32},{32,36}... | collective-permute-start | bytes 196616 | tf_op jit(solution)/shard_map/ppermute | solution.py:21
  29.9 1.0 gather_fusion.1
  31.0 1.9 collective-permute-start.1
  33.4 5.3 %collective-permute-done.1 = f32[32,512]{0,1:T(8,128)S(1)} collective-permute-done((f32[32,512]{0,1:T(8,128)S(1)}, f32[32,512]{0,1:T(8,128)S(1)}, u32[]{:S(2)}, u32[]{:S(2)}) %collective-permute-start.1) | collective-permute-done | bytes 65568 | tf_op jit(solution)/shard_map/ppermute | solution.py:21
  38.8 11.7 %fusion.1 = f32[32,768]{1,0:T(8,128)S(1)} fusion(f32[1,768,3072]{2,1,0:T(8,128)} %param.7, s32[768]{0:T(1024)S(1)} %iota_add_fusion, f32[32,512]{1,0:T(8,128)S(1)} %copy.14, f32[32,512]{1,0:T(8,128)S(1)} %copy.13, f32[32,2048]{1,0:T(8,128)S(1)} %copy.12), kind=kOutput, calls=%fused_computation.5 | convolution fusion | flops 913244160 | bytes 9931776 | tf_op jit(solution)/shard_map/dot_general | solution.py:25
  50.6 7.4 %fusion = f32[32,3072]{1,0:T(8,128)} fusion(f32[32,768]{1,0:T(8,128)S(1)} %fusion.1, f32[1,768,3072]{2,1,0:T(8,128)S(1)} %copy-done, s32[768]{0:T(1024)S(1)} %iota_add_fusion), kind=kOutput, calls=%fused_computation.4 | convolution fusion | flops 913047552 | bytes 9931776 | tf_op jit(solution)/shard_map/dot_general | solution.py:57
  58.1 50.1 %all-reduce.2.cloned.1.call-done = f32[32,3072]{1,0:T(8,128)} async-done(((f32[32,3072]{1,0:T(8,128)}), f32[32,3072]{1,0:T(8,128)}) %all-reduce.2.cloned.1.call-update) | async-done | bytes 393232 | tf_op jit(solution)/shard_map/psum | solution.py:58
  108.2 0.9 fusion.29
  109.1 5.8 %collective-permute-start.3 = (f32[32,512]{1,0:T(8,128)S(1)}, f32[32,512]{1,0:T(8,128)S(1)}, u32[]{:S(2)}, u32[]{:S(2)}) collective-permute-start(f32[32,512]{1,0:T(8,128)S(1)} %get-tuple-element.11), channel_id=1, source_target_pairs={{0,4},{4,8},{8,12},{12,16},{16,20},{20,24},{24,28},{28,32},{32,36}... | collective-permute-start | bytes 196616 | tf_op jit(solution)/shard_map/ppermute | solution.py:21
  114.9 2.1 collective-permute-start.2
  117.5 3.0 collective-permute-done.2
  120.5 1.4 fusion.4
  122.2 80.5 %psum.22 = f32[96,32]{0,1:T(8,128)S(1)} all-reduce(f32[96,32]{0,1:T(8,128)S(1)} %convolution_bitcast_fusion.2), channel_id=1, replica_groups=mesh['sub'=64,'row'=4] {'sub','row'}, use_global_device_ids=true, to_apply=%region_1.3 | all-reduce | flops 3072 | bytes 24576 | tf_op jit(solution)/shard_map/psum | solution.py:72
  203.3 72.9 %psum.23 = f32[96,32]{0,1:T(8,128)S(1)} all-reduce(f32[96,32]{0,1:T(8,128)S(1)} %convolution_bitcast_fusion.1), channel_id=1, replica_groups=mesh['sub'=64,'row'=4] {'sub','row'}, use_global_device_ids=true, to_apply=%region_2.4 | all-reduce | flops 3072 | bytes 24576 | tf_op jit(solution)/shard_map/psum | solution.py:33
  276.3 0.8 fusion.31
  277.8 112.5 %all-gather.4.cloned.1.call-done = f32[8192,32]{1,0:T(8,128)} async-done(((f32[32,32]{1,0:T(8,128)}), f32[8192,32]{1,0:T(8,128)}) %all-gather.4.cloned.1.call-update) | async-done | bytes 1048592 | tf_op jit(solution)/shard_map/all_gather | solution.py:11
  390.3 2.5 reduce_sum.11
  392.9 2.9 cholesky.18
  397.2 2.4 custom-call.7
  399.9 0.7 copy.17
  (36 shorter events, 5.5 us)
Async XLA Ops:
  7.2 101.0 %all-reduce.2.cloned.1.call-start = ((), (), s32[]{:S(2)}) async-start(), calls=%async_computation | async-start | bytes 786432 | tf_op jit(solution)/shard_map/psum | solution.py:58
  24.6 8.6 %collective-permute-start = (f32[32,512]{0,1:T(8,128)S(1)}, f32[32,512]{0,1:T(8,128)S(1)}, u32[]{:S(2)}, u32[]{:S(2)}) collective-permute-start(f32[32,512]{0,1:T(8,128)S(1)} %select_bitcast_fusion.1), channel_id=1, source_target_pairs={{0,4},{4,8},{8,12},{12,16},{16,20},{20,24},{24,28},{28,32},{32,36}... | collective-permute-start | bytes 196616 | tf_op jit(solution)/shard_map/ppermute | solution.py:21
  31.0 7.7 %collective-permute-start.1 = (f32[32,512]{0,1:T(8,128)S(1)}, f32[32,512]{0,1:T(8,128)S(1)}, u32[]{:S(2)}, u32[]{:S(2)}) collective-permute-start(f32[32,512]{0,1:T(8,128)S(1)} %select_bitcast_fusion), channel_id=1, source_target_pairs={{4,0},{8,4},{12,8},{16,12},{20,16},{24,20},{28,24},{32,28},{36,32}... | collective-permute-start | bytes 196616 | tf_op jit(solution)/shard_map/ppermute | solution.py:21
  38.8 11.8 %copy-start = (f32[1,768,3072]{2,1,0:T(8,128)S(1)}, f32[1,768,3072]{2,1,0:T(8,128)}, u32[]{:S(2)}) copy-start(f32[1,768,3072]{2,1,0:T(8,128)} %param.7) | copy-start | bytes 28311556
  38.8 83.0 %copy-start.1 = (f32[96,1,512]{2,1,0:T(1,128)S(1)}, f32[96,1,512]{2,1,0:T(1,128)}, u32[]{:S(2)}) copy-start(f32[96,1,512]{2,1,0:T(1,128)} %param.8) | copy-start | bytes 589828
  58.0 332.3 %all-gather.4.cloned.1.call-start = ((), (), s32[]{:S(2)}) async-start(), calls=%async_computation.1 | async-start | bytes 4210688 | tf_op jit(solution)/shard_map/all_gather | solution.py:11
  109.1 8.0 %collective-permute-start.3 = (f32[32,512]{1,0:T(8,128)S(1)}, f32[32,512]{1,0:T(8,128)S(1)}, u32[]{:S(2)}, u32[]{:S(2)}) collective-permute-start(f32[32,512]{1,0:T(8,128)S(1)} %get-tuple-element.11), channel_id=1, source_target_pairs={{0,4},{4,8},{8,12},{12,16},{16,20},{20,24},{24,28},{28,32},{32,36}... | collective-permute-start | bytes 196616 | tf_op jit(solution)/shard_map/ppermute | solution.py:21
  114.9 5.6 %collective-permute-start.2 = (f32[32,512]{1,0:T(8,128)S(1)}, f32[32,512]{1,0:T(8,128)S(1)}, u32[]{:S(2)}, u32[]{:S(2)}) collective-permute-start(f32[32,512]{1,0:T(8,128)S(1)} %get-tuple-element.10), channel_id=1, source_target_pairs={{4,0},{8,4},{12,8},{16,12},{20,16},{24,20},{28,24},{32,28},{36,32}... | collective-permute-start | bytes 196616 | tf_op jit(solution)/shard_map/ppermute | solution.py:21
Sparse Core Ops, SparseCore 0:
  58.2 49.9 all-reduce.1
  277.3 112.9 all-gather.3
